TPU v7x, 512 devices: a whole 4x4x16 slice. The times are simulated.
512 devices in a mesh: req: 128 (over z, y, core), wt: 4 (over x).
Axes of the slice: x: 4, y: 4, z: 16, core: 2. Of those that a mesh axis runs over, the one named last changes fastest.
Arguments:
- hidden_in: bfloat16 [32768, 5120], P('req', 'wt'), may hold values from -6 to 6
- queries: bfloat16 [32768, 5120], P('req', 'wt'), as said below
- key_proj: bfloat16 [32768, 5120], P('req', 'wt'), as said below
- values: bfloat16 [32768, 5120], P('req', 'wt'), may hold values from -6 to 6
- query_gain: float32 [5120], P('wt'), may hold values from 0.1 to 1.9
- key_gain: float32 [5120], P('wt'), may hold values from 0.1 to 1.9
- attn_gain: float32 [5120], P('wt'), may hold values from 0.1 to 1.9
- gate_w: bfloat16 [5120, 13824], P('wt', 'req'), may hold values from -0.078125 to 0.078125
- up_w: bfloat16 [5120, 13824], P('wt', 'req'), may hold values from -0.078125 to 0.078125
- lengths: int32 [128], replicated, may hold values from 1 to 256, 4608 in all
- assign: int32 [128], replicated, may hold values from 0 to 127, each once
- page_table: int32 [128, 2], P('req'), may hold values from 0 to 1, each once within a row
Outputs:
- gated: bfloat16 [128, 36, 13824], P(None, 'wt', 'req')
- key_cache: bfloat16 [256, 128, 5120], P('req', None, 'wt')
- value_cache: bfloat16 [256, 128, 5120], P('req', None, 'wt')
Inputs may be any that keep to these rules, and one draw needn't show every extreme that they name: lengths sum to 4608 and at least one request has exactly 256 tokens. `assign`: each device of req serves exactly one request. `page_table`: each row names each of the 2 pages of one device once. `queries`: real-valued entries within -24 to 24. `key_proj`: real-valued entries within -24 to 24.
All inputs are finite; a program needn't handle non-finite values.
Results may differ from a plain program's by a relative error of at most 0.013.
Values may be sent and summed in bfloat16 or wider, within the bound.
No kernel may reach another device: no remote copies, remote signals or barrier semaphores. Data moves between devices by JAX's collectives and lax.ppermute only.
A program may use at most 128 MiB of HBM per device.

v0:
```python
import jax
import jax.numpy as jnp
from jax import lax
from jax.sharding import Mesh, PartitionSpec as P

D = 5120
HD = 128
PAGE = 128
LIVE = 36
EPS = 1e-06
THETA = 500000.0


def rope_tables(row_count, head_width):
    half_width = head_width // 2
    frequency = THETA ** (-(jnp.arange(half_width, dtype=jnp.float32) * 2.0 / head_width))
    angles = jnp.arange(row_count, dtype=jnp.float32)[:, None] * frequency[None, :]
    return (jnp.cos(angles), jnp.sin(angles))


def rotate(heads_in, cosine, sine_table):
    half_width = heads_in.shape[-1] // 2
    leading = heads_in[..., :half_width]
    trailing = heads_in[..., half_width:]
    cos_b = cosine[:, None, :]
    sin_b = sine_table[:, None, :]
    return jnp.concatenate(
        [leading * cos_b - trailing * sin_b, trailing * cos_b + leading * sin_b], axis=-1
    )


def deal_rows(source, owner_start, owner_len, device, owners, live_rows):
    slot_count = source.shape[0]
    feature_count = source.shape[1]
    per_peer = slot_count // owners
    column = jnp.arange(per_peer, dtype=jnp.int32)[None, :]
    target_dev = jnp.arange(owners, dtype=jnp.int32)[:, None]
    my_start = owner_start[device]
    my_length = owner_len[device]
    local_index = (target_dev - my_start) % owners + owners * column
    usable = local_index < my_length
    picked = jnp.where(
        usable[:, :, None],
        source[jnp.minimum(local_index, slot_count - 1)],
        jnp.zeros((), source.dtype),
    )
    arrived = lax.all_to_all(picked, ("ra", "rb"), split_axis=0, concat_axis=0, tiled=True)
    src_start = owner_start[:, None]
    src_length = owner_len[:, None]
    sent_index = (device - src_start) % owners + owners * column
    landing = jnp.where(
        sent_index < src_length, (src_start + sent_index - device) // owners, live_rows
    )
    packed = jnp.zeros((live_rows, feature_count), source.dtype)
    return packed.at[landing.reshape(-1)].set(arrived.reshape(-1, feature_count), mode="drop")


def per_device(
    hidden_in,
    queries,
    key_proj,
    values,
    query_gain,
    key_gain,
    attn_gain,
    gate_w,
    up_w,
    lengths,
    assign,
    page_table,
):
    slot_count = hidden_in.shape[0]
    feature_count = hidden_in.shape[1]
    owners = lax.axis_size(("ra", "rb"))
    device = lax.axis_index("ra") * lax.axis_size("rb") + lax.axis_index("rb")
    head_count = feature_count // HD
    unit_count = gate_w.shape[1]
    owner_req = jnp.zeros((owners,), jnp.int32).at[assign].set(jnp.arange(owners, dtype=jnp.int32))
    starts = jnp.cumsum(lengths) - lengths
    owner_start = starts[owner_req]
    owner_len = lengths[owner_req]
    my_length = owner_len[device]
    query_f = queries.astype(jnp.float32)
    key_f = key_proj.astype(jnp.float32)
    query_sq, key_sq = lax.psum(
        (jnp.sum(query_f * query_f, axis=1), jnp.sum(key_f * key_f, axis=1)), "wt"
    )
    query_n = query_f * lax.rsqrt(query_sq / D + EPS)[:, None] * query_gain
    key_n = key_f * lax.rsqrt(key_sq / D + EPS)[:, None] * key_gain
    cosine, sine_table = rope_tables(slot_count, HD)
    query_r = rotate(query_n.reshape(slot_count, head_count, HD), cosine, sine_table).astype(
        jnp.bfloat16
    )
    key_r = rotate(key_n.reshape(slot_count, head_count, HD), cosine, sine_table).astype(
        jnp.bfloat16
    )
    scores = jnp.einsum(
        "qhd,khd->hqk", query_r, key_r, preferred_element_type=jnp.float32
    ) * HD ** (-0.5)
    position = jnp.arange(slot_count, dtype=jnp.int32)
    allowed = (position[None, :] <= position[:, None]) & (position[None, :] < my_length)
    scores = jnp.where(allowed[None], scores, -jnp.inf)
    row_peak = jnp.max(scores, axis=2, keepdims=True)
    expd = jnp.exp(scores - row_peak)
    probabilities = (expd / jnp.sum(expd, axis=2, keepdims=True)).astype(jnp.bfloat16)
    value_heads = values.reshape(slot_count, head_count, HD)
    attended = jnp.einsum(
        "hqk,khd->qhd", probabilities, value_heads, preferred_element_type=jnp.float32
    )
    attended = attended.astype(jnp.bfloat16).reshape(slot_count, feature_count)
    attended_f = attended.astype(jnp.float32)
    attn_sq = lax.psum(jnp.sum(attended_f * attended_f, axis=1), "wt")
    layer_rows = (
        hidden_in.astype(jnp.float32)
        + attended_f * lax.rsqrt(attn_sq / D + EPS)[:, None] * attn_gain
    ).astype(jnp.bfloat16)
    live_mask = (position < my_length)[:, None]
    page_count = slot_count // PAGE
    zero_value = jnp.zeros((), jnp.bfloat16)
    key_pages = jnp.where(live_mask, key_r.reshape(slot_count, feature_count), zero_value).reshape(
        page_count, PAGE, feature_count
    )
    value_pages = jnp.where(live_mask, values, zero_value).reshape(page_count, PAGE, feature_count)
    placement = page_table[0]
    key_cache = jnp.zeros_like(key_pages).at[placement].set(key_pages)
    value_cache = jnp.zeros_like(value_pages).at[placement].set(value_pages)
    regrouped = deal_rows(layer_rows, owner_start, owner_len, device, owners, LIVE)
    outer = lax.axis_size("ra")
    inner = lax.axis_size("rb")
    piece = lax.all_gather(regrouped, "ra", axis=0, tiled=True)
    weights = lax.all_gather(jnp.stack([gate_w, up_w]), "rb", axis=2, tiled=True)
    stacked = jnp.einsum("tk,skn->tsn", piece, weights, preferred_element_type=jnp.float32)
    stacked = stacked.reshape(outer, LIVE, 2, inner * unit_count)
    summed = lax.psum_scatter(stacked, "wt", scatter_dimension=1, tiled=True)
    gated = (jax.nn.silu(summed[:, :, 0]) * summed[:, :, 1]).astype(jnp.bfloat16)
    rows_here = gated.shape[1]
    gated = gated.reshape(outer, rows_here, inner, unit_count)
    gated = lax.all_to_all(gated, "rb", split_axis=2, concat_axis=2, tiled=True)
    gated = jnp.transpose(gated, (0, 2, 1, 3)).reshape(outer * inner, rows_here, unit_count)
    return (gated, key_cache, value_cache)


def solution(mesh):
    inner = 4
    outer = mesh.shape["req"] // inner
    split = Mesh(mesh.devices.reshape(outer, inner, mesh.shape["wt"]), ("ra", "rb", "wt"))
    req = ("ra", "rb")
    placed = (
        P(req, "wt"),
        P(req, "wt"),
        P(req, "wt"),
        P(req, "wt"),
        P("wt"),
        P("wt"),
        P("wt"),
        P("wt", req),
        P("wt", req),
        P(),
        P(),
        P(req, None),
    )
    return jax.shard_map(
        per_device,
        mesh=split,
        in_specs=placed,
        out_specs=(P(None, "wt", req), P(req, None, "wt"), P(req, None, "wt")),
        check_vma=False,
    )
```

profile of v0, /device:TPU:1, one launch (start us, length us, event | category | flops | bytes accessed | tf_op | source)
XLA Modules:
  0.0 409.6 jit_solution(2444078418245778688)
XLA Ops:
  7.7 1.3 copy.84
  9.7 9.3 %all-reduce = (f32[256]{0:T(256)S(1)}, f32[256]{0:T(256)S(1)}) all-reduce(f32[256]{0:T(256)S(1)} %fusion.7, f32[256]{0:T(256)S(1)} %fusion.5), channel_id=1, replica_groups=mesh['ra'=32,'rb'=4,'wt'=4] {'wt'}, use_global_device_ids=true, to_apply=%region_5.6 | all-reduce | flops 512 | bytes 4096 | tf_op jit(solution)/shard_map/psum | solution.py:85
  19.8 0.9 fusion.40
  21.2 1.5 copy.110
  23.2 1.2 compare_select_fusion.4
  24.9 1.1 scatter_custom_fusion
  26.1 1.7 gather_fusion.1
  27.8 1.2 dynamic_slice.8
  32.2 1.5 copy.107
  33.7 2.6 copy.108
  36.3 1.1 copy.90
  40.1 2.7 fusion.42
  42.8 2.1 multiply_reduce_fusion
  45.4 6.0 %psum.23 = f32[256]{0:T(256)S(1)} all-reduce(f32[256]{0:T(256)S(1)} %get-tuple-element.33), channel_id=1, replica_groups=mesh['ra'=32,'rb'=4,'wt'=4] {'wt'}, use_global_device_ids=true, to_apply=%region_9.10 | all-reduce | flops 256 | bytes 2048 | tf_op jit(solution)/shard_map/psum | solution.py:112
  51.8 1.2 gather_fusion
  54.8 1.2 gather_fusion.2
  57.5 1.5 broadcast_select_fusion
  59.0 23.6 %all-to-all-start = ((bf16[128,2,1280]{2,1,0:T(2,128)(2,1)}), bf16[128,2,1280]{2,1,0:T(2,128)(2,1)S(1)}, u32[]{:S(2)}, u32[]{:S(2)}) async-start(bf16[128,2,1280]{2,1,0:T(2,128)(2,1)} %broadcast_select_fusion), calls=%async_computation | async-start | bytes 1310720 | tf_op jit(solution)/shard_map/all_to_all | solution.py:47
  83.3 35.7 %all-to-all-done = bf16[128,2,1280]{2,1,0:T(2,128)(2,1)S(1)} async-done(((bf16[128,2,1280]{2,1,0:T(2,128)(2,1)}), bf16[128,2,1280]{2,1,0:T(2,128)(2,1)S(1)}, u32[]{:S(2)}, u32[]{:S(2)}) %all-to-all-start) | async-done | bytes 655392 | tf_op jit(solution)/shard_map/all_to_all | solution.py:47
  119.3 2.2 scatter_custom_fusion.1
  121.7 1.2 copy.93
  123.0 140.6 %all-gather.6.cloned.1.call-done = bf16[32,36,1280]{2,1,0:T(8,128)(2,1)} async-done(((bf16[1,36,1280]{2,1,0:T(8,128)(2,1)}), bf16[32,36,1280]{2,1,0:T(8,128)(2,1)}) %all-gather.6.cloned.1.call-update) | async-done | bytes 2949136 | tf_op jit(solution)/shard_map/all_gather | solution.py:130
  263.5 3.7 reshape.493
  267.2 41.0 %all-gather.4.cloned.1.call-done = bf16[2,1280,432]{1,0,2:T(2,128)(2,1)} async-done(((bf16[2,1280,108]{1,0,2:T(2,128)(2,1)}), bf16[2,1280,432]{1,0,2:T(2,128)(2,1)}) %all-gather.4.cloned.1.call-update) | async-done | bytes 2211856 | tf_op jit(solution)/shard_map/all_gather | solution.py:131
  308.2 6.6 %fusion.1 = f32[1152,2,432]{0,2,1:T(8,128)} fusion(bf16[1152,1280,1]{1,0,2:T(8,128)(2,1)S(1)} %reshape.493, bf16[2,1280,432]{1,0,2:T(2,128)(2,1)} %all-gather.4.cloned.1.call-done), kind=kOutput, calls=%fused_computation.11 | convolution fusion | flops 2548039680 | bytes 9142272 | tf_op jit(solution)/shard_map/tk,skn->tsn/dot_general | solution.py:132
  314.8 7.9 %copy.95 = f32[1152,2,432]{2,1,0:T(2,128)} copy(f32[1152,2,432]{0,2,1:T(8,128)} %fusion.1) | data formatting | bytes 7962624 | tf_op jit(solution)/shard_map/tk,skn->tsn/dot_general | solution.py:132
  322.7 7.2 %copy.96 = f32[32,36,2,432]{3,0,2,1:T(8,128)} copy(f32[32,36,2,432]{3,2,1,0:T(2,128)} %bitcast.35) | data formatting | bytes 7962624 | tf_op jit(solution)/shard_map/reshape | solution.py:133
  329.9 1.1 copy-done.8
  332.7 56.7 %reduce-scatter.2.cloned.1.call-done = f32[32,9,2,432]{3,0,2,1:T(8,128)} async-done(((f32[32,36,2,432]{3,0,2,1:T(8,128)}), f32[32,9,2,432]{3,0,2,1:T(8,128)}) %reduce-scatter.2.cloned.1.call-update) | async-done | bytes 995344 | tf_op jit(solution)/shard_map/reduce_scatter | solution.py:134
  389.4 1.4 fusion.41
  392.4 4.0 all-to-all-start.1
  398.1 3.9 all-to-all-done.1
  (108 shorter events, 20.3 us)
Async XLA Ops:
  7.2 2.1 copy-start.9
  9.1 10.5 %copy-start.15 = (f32[1280]{0:T(1024)S(1)}, f32[1280]{0:T(1024)}, u32[]{:S(2)}) copy-start(f32[1280]{0:T(1024)} %param.17) | copy-start | bytes 15364
  21.2 4.9 %copy-start = (s32[128]{0:T(128)S(1)}, s32[128]{0:T(128)}, u32[]{:S(2)}) copy-start(s32[128]{0:T(128)} %param.21) | copy-start | bytes 1540
  21.2 9.1 %copy-start.16 = (f32[1280]{0:T(1024)S(1)}, f32[1280]{0:T(1024)}, u32[]{:S(2)}) copy-start(f32[1280]{0:T(1024)} %param.16) | copy-start | bytes 15364
  29.5 0.7 copy-start.19
  33.7 2.6 copy-start.3
  37.4 1.3 copy-start.2
  37.7 1.4 copy-start.1
  39.2 0.8 copy-start.7
  39.2 0.9 copy-start.14
  40.1 2.7 copy-start.10
  44.9 9.4 %copy-start.18 = (s32[2]{0:T(128)S(1)}, s32[2]{0:T(128)}, u32[]{:S(2)}) copy-start(s32[2]{0:T(128)} %iota_multiply_fusion.1) | copy-start | bytes 28
  44.9 9.6 %copy-start.11 = (bf16[256,1280]{1,0:T(8,128)(2,1)S(1)}, bf16[256,1280]{1,0:T(8,128)(2,1)}, u32[]{:S(2)}) copy-start(bf16[256,1280]{1,0:T(8,128)(2,1)} %param.12) | copy-start | bytes 1966084
  45.0 9.6 %copy-start.17 = (f32[1280]{0:T(1024)S(1)}, f32[1280]{0:T(1024)}, u32[]{:S(2)}) copy-start(f32[1280]{0:T(1024)} %param.18) | copy-start | bytes 15364
  56.1 0.6 copy-start.21
  59.0 62.6 %copy-start.12 = (bf16[1280,108]{0,1:T(8,128)(2,1)S(1)}, bf16[1280,108]{0,1:T(8,128)(2,1)}, u32[]{:S(2)}) copy-start(bf16[1280,108]{0,1:T(8,128)(2,1)} %param.20) | copy-start | bytes 829444
  59.0 62.6 %copy-start.13 = (bf16[1280,108]{0,1:T(8,128)(2,1)S(1)}, bf16[1280,108]{0,1:T(8,128)(2,1)}, u32[]{:S(2)}) copy-start(bf16[1280,108]{0,1:T(8,128)(2,1)} %param.19) | copy-start | bytes 829444
  59.0 60.1 %all-to-all-start = ((bf16[128,2,1280]{2,1,0:T(2,128)(2,1)}), bf16[128,2,1280]{2,1,0:T(2,128)(2,1)S(1)}, u32[]{:S(2)}, u32[]{:S(2)}) async-start(bf16[128,2,1280]{2,1,0:T(2,128)(2,1)} %broadcast_select_fusion), calls=%async_computation | async-start | bytes 1310720 | tf_op jit(solution)/shard_map/all_to_all | solution.py:47
  82.6 180.9 %all-gather.6.cloned.1.call-start = ((), (), s32[]{:S(2)}) async-start(), calls=%async_computation.5 | async-start | bytes 3379200 | tf_op jit(solution)/shard_map/all_gather | solution.py:130
  121.5 186.7 %all-gather.4.cloned.1.call-start = ((), (), s32[]{:S(2)}) async-start(), calls=%async_computation.3 | async-start | bytes 2764800 | tf_op jit(solution)/shard_map/all_gather | solution.py:131
  122.9 266.5 %reduce-scatter.2.cloned.1.call-start = ((), (), s32[]{:S(2)}) async-start(), calls=%async_computation.4 | async-start | bytes 5898240 | tf_op jit(solution)/shard_map/reduce_scatter | solution.py:134
  329.9 1.1 copy-start.8
  331.0 1.4 copy-start.4
  331.0 1.5 copy-start.20
  391.5 4.9 %copy-start.22 = (s32[1,2]{1,0:T(1,128)S(1)}, s32[1,2]{1,0:T(1,128)}, u32[]{:S(2)}) copy-start(s32[1,2]{1,0:T(1,128)} %param.23) | copy-start | bytes 28
  392.4 9.6 %all-to-all-start.1 = ((bf16[32,9,4,108]{3,0,1,2:T(8,128)(2,1)}), bf16[32,9,4,108]{3,0,1,2:T(8,128)(2,1)S(1)}, u32[]{:S(2)}, u32[]{:S(2)}) async-start(bf16[32,9,4,108]{3,0,1,2:T(8,128)(2,1)} %fusion.16), calls=%async_computation.2 | async-start | bytes 589824 | tf_op jit(solution)/shard_map/all_to_all | solution.py:138
  397.3 0.8 copy-start.6
  398.1 5.0 %copy-start.5 = (bf16[2,128,1280]{2,1,0:T(8,128)(2,1)}, bf16[2,128,1280]{2,1,0:T(8,128)(2,1)S(1)}, u32[]{:S(2)}) copy-start(bf16[2,128,1280]{2,1,0:T(8,128)(2,1)S(1)} %scatter_fusion.1) | copy-start | bytes 1966084
Sparse Core Ops, SparseCore 0:
  121.7 141.8 all-gather.5
  266.2 41.9 all-gather.3
  330.0 59.3 reduce-scatter.1
where the time goes:
time: 411 us; the launch traced here: 410 us
  waiting for transfers between devices  278 us (68%)
  local copies, waits for them, and re-layouts  50.9 us (12%)
  starting transfers between devices  27.8 us (7%)
  blocking collectives  15.3 us (4%)
  between operations  14.2 us (3%)
  other arithmetic  12.1 us (3%)
  matrix products  11.4 us (3%)
    all_gather x1, waiting for transfers between devices, per_device(): piece = lax.all_gather(regrouped, 'ra', axis=0, tiled=True)  141 us
    reduce_scatter x1, waiting for transfers between devices, per_device(): summed = lax.psum_scatter(stacked, 'wt', scatter_dimension=1, tiled=True)  56.7 us
    all_gather x1, waiting for transfers between devices, per_device(): lax.all_gather(jnp.stack([gate_w, up_w]), 'rb', axis=2, tiled=True)  41 us
    all_to_all x1, waiting for transfers between devices, deal_rows(): lax.all_to_all(picked, ('ra', 'rb'), split_axis=0, concat_axis=0, tiled=T...  35.7 us
    all_to_all x1, starting transfers between devices, deal_rows(): lax.all_to_all(picked, ('ra', 'rb'), split_axis=0, concat_axis=0, tiled=T...  23.6 us
    unnamed x55, local copies, waits for them, and re-layouts  16.3 us
    psum x1, blocking collectives, per_device(): lax.psum((jnp.sum(query_f * query_f, axis=1), jnp.sum(key_f * key_f, axis...  9.29 us
  transfers between devices with their start and end apart: 5, of which 5 were waited for; matrix products, arithmetic and copies ran while one was open for 2% of the time, Pallas kernels for 0%

commit v1 on v0

--- a/solution.py
+++ b/solution.py
@@ -127,7 +127,8 @@
     regrouped = deal_rows(layer_rows, owner_start, owner_len, device, owners, LIVE)
     outer = lax.axis_size("ra")
     inner = lax.axis_size("rb")
-    piece = lax.all_gather(regrouped, "ra", axis=0, tiled=True)
+    sent = jnp.stack([regrouped] * lax.axis_size("ra"))
+    piece = jnp.concatenate(lax.all_to_all(sent, "ra", 0, 0), axis=0)
     weights = lax.all_gather(jnp.stack([gate_w, up_w]), "rb", axis=2, tiled=True)
     stacked = jnp.einsum("tk,skn->tsn", piece, weights, preferred_element_type=jnp.float32)
     stacked = stacked.reshape(outer, LIVE, 2, inner * unit_count)

time: 411 us -> 359 us (0.87)
  waiting for transfers between devices: 278 us -> 235 us
  local copies, waits for them, and re-layouts: 50.9 us -> 34.3 us
  starting transfers between devices: 27.8 us -> 34.4 us
    all_gather x1 -> x0, waiting for transfers between devices: 141 us -> none  [per_device(): piece = lax.all_gather(regrouped, 'ra', axis=0, tiled=True)]
    all_to_all x0 -> x1, waiting for transfers between devices: none -> 98.9 us  [per_device(): piece = jnp.concatenate(lax.all_to_all(sent, 'ra', 0, 0), axis=0)]
    dot_general x1 -> x0, local copies, waits for them, and re-layouts: 7.91 us -> none  [per_device(): jnp.einsum('tk,skn->tsn', piece, weights, preferred_element_type=jnp.floa...]
    reshape x1 -> x0, local copies, waits for them, and re-layouts: 7.21 us -> none  [per_device(): stacked = stacked.reshape(outer, LIVE, 2, inner * unit_count)]
    all_to_all x0 -> x1, starting transfers between devices: none -> 6.75 us  [per_device(): piece = jnp.concatenate(lax.all_to_all(sent, 'ra', 0, 0), axis=0)]
    reduce_scatter x1, waiting for transfers between devices: 56.7 us -> 52.5 us  [per_device(): summed = lax.psum_scatter(stacked, 'wt', scatter_dimension=1, tiled=True)]
    unnamed x55 -> x50, local copies, waits for them, and re-layouts: 16.3 us -> 12.7 us
where the time goes in v1:
time: 359 us; the launch traced here: 358 us
  waiting for transfers between devices  235 us (65%)
  starting transfers between devices  34.4 us (10%)
  local copies, waits for them, and re-layouts  34.3 us (10%)
  blocking collectives  15.3 us (4%)
  between operations  14.5 us (4%)
  other arithmetic  12.9 us (4%)
  matrix products  11.4 us (3%)
    all_to_all x1, waiting for transfers between devices, per_device(): piece = jnp.concatenate(lax.all_to_all(sent, 'ra', 0, 0), axis=0)  98.9 us
    reduce_scatter x1, waiting for transfers between devices, per_device(): summed = lax.psum_scatter(stacked, 'wt', scatter_dimension=1, tiled=True)  52.5 us
    all_gather x1, waiting for transfers between devices, per_device(): lax.all_gather(jnp.stack([gate_w, up_w]), 'rb', axis=2, tiled=True)  44.1 us
    all_to_all x1, waiting for transfers between devices, deal_rows(): lax.all_to_all(picked, ('ra', 'rb'), split_axis=0, concat_axis=0, tiled=T...  35.8 us
    all_to_all x1, starting transfers between devices, deal_rows(): lax.all_to_all(picked, ('ra', 'rb'), split_axis=0, concat_axis=0, tiled=T...  23.5 us
    unnamed x50, local copies, waits for them, and re-layouts  12.7 us
    psum x1, blocking collectives, per_device(): lax.psum((jnp.sum(query_f * query_f, axis=1), jnp.sum(key_f * key_f, axis...  9.29 us
  transfers between devices with their start and end apart: 5, of which 5 were waited for; matrix products, arithmetic and copies ran while one was open for 2% of the time, Pallas kernels for 0%

profile of v1, /device:TPU:1, one launch (start us, length us, event | category | flops | bytes accessed | tf_op | source)
XLA Modules:
  0.0 357.9 jit_solution(16158160334510336585)
XLA Ops:
  7.7 1.3 copy.74
  9.7 9.3 %all-reduce = (f32[256]{0:T(256)S(1)}, f32[256]{0:T(256)S(1)}) all-reduce(f32[256]{0:T(256)S(1)} %fusion.9, f32[256]{0:T(256)S(1)} %fusion.7), channel_id=1, replica_groups=mesh['ra'=32,'rb'=4,'wt'=4] {'wt'}, use_global_device_ids=true, to_apply=%region_5.6 | all-reduce | flops 512 | bytes 4096 | tf_op jit(solution)/shard_map/psum | solution.py:85
  19.8 0.9 fusion.43
  21.2 1.5 copy.99
  23.2 1.2 compare_select_fusion.4
  24.9 1.1 scatter_custom_fusion
  26.0 1.8 gather_fusion.1
  27.8 1.3 dynamic_slice.8
  32.5 1.5 copy.96
  33.9 2.6 copy.97
  36.6 1.1 copy.80
  40.3 2.7 fusion.45
  43.1 2.1 multiply_reduce_fusion
  45.6 6.0 %psum.23 = f32[256]{0:T(256)S(1)} all-reduce(f32[256]{0:T(256)S(1)} %get-tuple-element.33), channel_id=1, replica_groups=mesh['ra'=32,'rb'=4,'wt'=4] {'wt'}, use_global_device_ids=true, to_apply=%region_9.10 | all-reduce | flops 256 | bytes 2048 | tf_op jit(solution)/shard_map/psum | solution.py:112
  52.1 1.2 gather_fusion
  55.1 1.2 gather_fusion.2
  57.9 1.5 broadcast_select_fusion
  59.4 23.5 %all-to-all-start = ((bf16[128,2,1280]{2,1,0:T(2,128)(2,1)}), bf16[128,2,1280]{2,1,0:T(2,128)(2,1)S(1)}, u32[]{:S(2)}, u32[]{:S(2)}) async-start(bf16[128,2,1280]{2,1,0:T(2,128)(2,1)} %broadcast_select_fusion), calls=%async_computation | async-start | bytes 1310720 | tf_op jit(solution)/shard_map/all_to_all | solution.py:47
  83.6 35.8 %all-to-all-done = bf16[128,2,1280]{2,1,0:T(2,128)(2,1)S(1)} async-done(((bf16[128,2,1280]{2,1,0:T(2,128)(2,1)}), bf16[128,2,1280]{2,1,0:T(2,128)(2,1)S(1)}, u32[]{:S(2)}, u32[]{:S(2)}) %all-to-all-start) | async-done | bytes 655392 | tf_op jit(solution)/shard_map/all_to_all | solution.py:47
  119.6 1.6 scatter_custom_fusion.1
  121.2 1.9 stack.8
  123.1 6.8 %all-to-all-start.1 = ((bf16[32,36,1280]{2,1,0:T(8,128)(2,1)}), bf16[32,36,1280]{2,1,0:T(8,128)(2,1)S(1)}, u32[]{:S(2)}, u32[]{:S(2)}) async-start(bf16[32,36,1280]{2,1,0:T(8,128)(2,1)} %stack.8), calls=%async_computation.1 | async-start | bytes 6553600 | tf_op jit(solution)/shard_map/all_to_all | solution.py:131
  129.9 1.1 pad_maximum_fusion
  131.1 1.2 copy.83
  132.4 44.1 %all-gather.2.cloned.1.call-done = bf16[2,1280,432]{1,0,2:T(2,128)(2,1)} async-done(((bf16[2,1280,108]{1,0,2:T(2,128)(2,1)}), bf16[2,1280,432]{1,0,2:T(2,128)(2,1)}) %all-gather.2.cloned.1.call-update) | async-done | bytes 2211856 | tf_op jit(solution)/shard_map/all_gather | solution.py:132
  176.4 98.9 %all-to-all-done.1 = bf16[32,36,1280]{2,1,0:T(8,128)(2,1)S(1)} async-done(((bf16[32,36,1280]{2,1,0:T(8,128)(2,1)}), bf16[32,36,1280]{2,1,0:T(8,128)(2,1)S(1)}, u32[]{:S(2)}, u32[]{:S(2)}) %all-to-all-start.1) | async-done | bytes 2949152 | tf_op jit(solution)/shard_map/all_to_all | solution.py:131
  275.3 6.5 %fusion.1 = f32[32,36,2,432]{3,0,2,1:T(8,128)} fusion(bf16[32,36,1280,1]{2,1,0,3:T(8,128)(2,1)S(1)} %bitcast.38, bf16[2,1280,432]{1,0,2:T(2,128)(2,1)} %all-gather.2.cloned.1.call-done), kind=kOutput, calls=%fused_computation.8 | convolution fusion | flops 2548039680 | bytes 9142272 | tf_op jit(solution)/shard_map/tk,skn->tsn/dot_general | solution.py:133
  281.8 1.1 copy-done.8
  284.7 52.5 %reduce-scatter.2.cloned.1.call-done = f32[32,9,2,432]{3,0,2,1:T(8,128)} async-done(((f32[32,36,2,432]{3,0,2,1:T(8,128)}), f32[32,9,2,432]{3,0,2,1:T(8,128)}) %reduce-scatter.2.cloned.1.call-update) | async-done | bytes 995344 | tf_op jit(solution)/shard_map/reduce_scatter | solution.py:135
  337.2 1.4 fusion.44
  340.5 4.0 %all-to-all-start.2 = ((bf16[32,9,4,108]{3,0,1,2:T(8,128)(2,1)}), bf16[32,9,4,108]{3,0,1,2:T(8,128)(2,1)S(1)}, u32[]{:S(2)}, u32[]{:S(2)}) async-start(bf16[32,9,4,108]{3,0,1,2:T(8,128)(2,1)} %copy.86), calls=%async_computation.3 | async-start | bytes 589824 | tf_op jit(solution)/shard_map/all_to_all | solution.py:139
  346.2 3.9 %all-to-all-done.2 = bf16[32,9,4,108]{3,0,1,2:T(8,128)(2,1)S(1)} async-done(((bf16[32,9,4,108]{3,0,1,2:T(8,128)(2,1)}), bf16[32,9,4,108]{3,0,1,2:T(8,128)(2,1)S(1)}, u32[]{:S(2)}, u32[]{:S(2)}) %all-to-all-start.2) | async-done | bytes 248864 | tf_op jit(solution)/shard_map/all_to_all | solution.py:139
  (102 shorter events, 20.8 us)
Async XLA Ops:
  7.2 2.1 copy-start.9
  9.0 10.5 %copy-start.13 = (f32[1280]{0:T(1024)S(1)}, f32[1280]{0:T(1024)}, u32[]{:S(2)}) copy-start(f32[1280]{0:T(1024)} %param.17) | copy-start | bytes 15364
  21.2 4.9 %copy-start = (s32[128]{0:T(128)S(1)}, s32[128]{0:T(128)}, u32[]{:S(2)}) copy-start(s32[128]{0:T(128)} %param.21) | copy-start | bytes 1540
  21.2 9.4 %copy-start.14 = (f32[1280]{0:T(1024)S(1)}, f32[1280]{0:T(1024)}, u32[]{:S(2)}) copy-start(f32[1280]{0:T(1024)} %param.16) | copy-start | bytes 15364
  29.8 0.7 copy-start.17
  33.9 2.6 copy-start.3
  37.7 1.3 copy-start.2
  38.0 1.4 copy-start.1
  39.5 0.8 copy-start.7
  39.5 0.9 copy-start.12
  40.3 2.7 copy-start.10
  45.2 9.4 %copy-start.16 = (s32[2]{0:T(128)S(1)}, s32[2]{0:T(128)}, u32[]{:S(2)}) copy-start(s32[2]{0:T(128)} %iota_multiply_fusion.1) | copy-start | bytes 28
  45.2 9.6 %copy-start.11 = (bf16[256,1280]{1,0:T(8,128)(2,1)S(1)}, bf16[256,1280]{1,0:T(8,128)(2,1)}, u32[]{:S(2)}) copy-start(bf16[256,1280]{1,0:T(8,128)(2,1)} %param.12) | copy-start | bytes 1966084
  45.2 9.6 %copy-start.15 = (f32[1280]{0:T(1024)S(1)}, f32[1280]{0:T(1024)}, u32[]{:S(2)}) copy-start(f32[1280]{0:T(1024)} %param.18) | copy-start | bytes 15364
  56.3 0.7 copy-start.19
  59.4 59.9 %all-to-all-start = ((bf16[128,2,1280]{2,1,0:T(2,128)(2,1)}), bf16[128,2,1280]{2,1,0:T(2,128)(2,1)S(1)}, u32[]{:S(2)}, u32[]{:S(2)}) async-start(bf16[128,2,1280]{2,1,0:T(2,128)(2,1)} %broadcast_select_fusion), calls=%async_computation | async-start | bytes 1310720 | tf_op jit(solution)/shard_map/all_to_all | solution.py:47
  123.1 152.2 %all-to-all-start.1 = ((bf16[32,36,1280]{2,1,0:T(8,128)(2,1)}), bf16[32,36,1280]{2,1,0:T(8,128)(2,1)S(1)}, u32[]{:S(2)}, u32[]{:S(2)}) async-start(bf16[32,36,1280]{2,1,0:T(8,128)(2,1)} %stack.8), calls=%async_computation.1 | async-start | bytes 6553600 | tf_op jit(solution)/shard_map/all_to_all | solution.py:131
  129.9 46.5 %all-gather.2.cloned.1.call-start = ((), (), s32[]{:S(2)}) async-start(), calls=%async_computation.4 | async-start | bytes 2764800 | tf_op jit(solution)/shard_map/all_gather | solution.py:132
  132.3 204.9 %reduce-scatter.2.cloned.1.call-start = ((), (), s32[]{:S(2)}) async-start(), calls=%async_computation.5 | async-start | bytes 5898240 | tf_op jit(solution)/shard_map/reduce_scatter | solution.py:135
  281.8 1.1 copy-start.8
  282.9 1.6 copy-start.4
  282.9 1.6 copy-start.18
  339.4 5.1 %copy-start.20 = (s32[1,2]{1,0:T(1,128)S(1)}, s32[1,2]{1,0:T(1,128)}, u32[]{:S(2)}) copy-start(s32[1,2]{1,0:T(1,128)} %param.23) | copy-start | bytes 28
  340.5 9.6 %all-to-all-start.2 = ((bf16[32,9,4,108]{3,0,1,2:T(8,128)(2,1)}), bf16[32,9,4,108]{3,0,1,2:T(8,128)(2,1)S(1)}, u32[]{:S(2)}, u32[]{:S(2)}) async-start(bf16[32,9,4,108]{3,0,1,2:T(8,128)(2,1)} %copy.86), calls=%async_computation.3 | async-start | bytes 589824 | tf_op jit(solution)/shard_map/all_to_all | solution.py:139
  345.3 0.8 copy-start.6
  346.2 5.0 %copy-start.5 = (bf16[2,128,1280]{2,1,0:T(8,128)(2,1)}, bf16[2,128,1280]{2,1,0:T(8,128)(2,1)S(1)}, u32[]{:S(2)}) copy-start(bf16[2,128,1280]{2,1,0:T(8,128)(2,1)S(1)} %scatter_fusion.1) | copy-start | bytes 1966084
Sparse Core Ops, SparseCore 0:
  133.4 42.9 all-gather.1
  282.0 55.2 reduce-scatter.1
